TPU v7x, 512 devices: a whole 4x8x8 slice. The times are simulated.
512 devices in a mesh: group: 8 (over z_lo, core), dp: 8 (over y), tensor: 8 (over z_hi, x).
Axes of the slice: x: 4, y: 8, z: 8 (z_hi: 2, z_lo: 4; z = z_hi * 4 + z_lo), core: 2. Of those that a mesh axis runs over, the one named last changes fastest.
Arguments:
- keyvalue_local: float32 [8, 2, 4096, 1024], P('group', None, 'dp', 'tensor'), may hold values from -6 to 6
- keyvalue_anchor: float32 [2, 4096, 1024], P(None, 'dp', 'tensor'), may hold values from -6 to 6
- keyvalue_state: float32 [2, 4096, 1024], P(None, 'dp', 'tensor'), may hold values from -6 to 6
- router_local: float32 [8, 4096, 8], P('group', 'dp'), may hold values from -6 to 6
- router_anchor: float32 [4096, 8], P('dp'), may hold values from -6 to 6
- router_state: float32 [4096, 8], P('dp'), may hold values from -6 to 6
- gain_local: float32 [8, 2, 4096], P('group', None, 'dp'), may hold values from -6 to 6
- gain_anchor: float32 [2, 4096], P(None, 'dp'), may hold values from -6 to 6
- gain_state: float32 [2, 4096], P(None, 'dp'), may hold values from -6 to 6
- embed_local: float32 [8, 1000, 4096], P('group', 'dp', 'tensor'), may hold values from -6 to 6
- embed_anchor: float32 [1000, 4096], P('dp', 'tensor'), may hold values from -6 to 6
- embed_state: float32 [1000, 4096], P('dp', 'tensor'), may hold values from -6 to 6
- embed_basis: float32 [4096, 64], P('tensor'), may hold values from -0.25 to 0.25
- outer_rate: float32 [], replicated, may hold values from 0.5 to 1
Outputs:
- keyvalue_average: float32 [2, 4096, 1024], P(None, 'dp', 'tensor')
- keyvalue_momentum: float32 [2, 4096, 1024], P(None, 'dp', 'tensor')
- keyvalue_updated: float32 [2, 4096, 1024], P(None, 'dp', 'tensor')
- router_average: float32 [4096, 8], P('dp')
- router_momentum: float32 [4096, 8], P('dp')
- router_updated: float32 [4096, 8], P('dp')
- gain_average: float32 [2, 4096], P(None, 'dp')
- gain_momentum: float32 [2, 4096], P(None, 'dp')
- gain_updated: float32 [2, 4096], P(None, 'dp')
- embed_average: float32 [1000, 4096], P('dp', 'tensor')
- embed_momentum: float32 [1000, 4096], P('dp', 'tensor')
- embed_updated: float32 [1000, 4096], P('dp', 'tensor')
All inputs are finite; a program needn't handle non-finite values.
Results may differ from a plain program's by a relative error of at most 0.0001.
Values sent between devices are 32-bit elements; how exact they have to be, the bound alone decides.
No kernel may reach another device: no remote copies, remote signals or barrier semaphores. Data moves between devices by JAX's collectives and lax.ppermute only.
A program may use at most 64 MiB of HBM per device.

v0:
```python
import jax
import jax.numpy as jnp
from jax import lax
from jax.sharding import PartitionSpec as P

HIGHEST = lax.Precision.HIGHEST
MODE = "separate"


def nesterov(average, state, anchor, outer_rate):
    momentum = 0.5 * state + average
    updated = anchor - outer_rate * (average + 0.5 * momentum)
    return (average, momentum, updated)


def local(
    kv_local,
    kv_anchor,
    kv_state,
    r_local,
    r_anchor,
    r_state,
    g_local,
    g_anchor,
    g_state,
    e_local,
    e_anchor,
    e_state,
    basis,
    rate,
):
    groups = lax.axis_size("group")
    kv_diff = kv_anchor - kv_local[0]
    r_diff = r_anchor - r_local[0]
    g_diff = g_anchor - g_local[0]
    partial = jnp.dot(
        e_anchor - e_local[0], basis, precision=HIGHEST, preferred_element_type=jnp.float32
    )
    if MODE == "concat":
        partial = lax.psum(partial, "tensor")
        pieces = (kv_diff, r_diff, g_diff, partial)
        flat = jnp.concatenate([p.reshape(-1) for p in pieces])
        total = lax.psum(flat, "group")
        sums, at = ([], 0)
        for p in pieces:
            sums.append(total[at : at + p.size].reshape(p.shape))
            at += p.size
        kv_sum, r_sum, g_sum, factors = sums
    elif MODE == "separate":
        partial = lax.psum(partial, "tensor")
        kv_sum, r_sum, g_sum, factors = lax.psum((kv_diff, r_diff, g_diff, partial), "group")
    elif MODE == "nested":
        kv_sum, r_sum, g_sum = lax.psum((kv_diff, r_diff, g_diff), "group")
        factors = lax.psum(lax.psum(partial, "tensor"), "group")
    kv_out = nesterov(kv_sum / groups, kv_state, kv_anchor, rate)
    r_out = nesterov(r_sum / groups, r_state, r_anchor, rate)
    g_out = nesterov(g_sum / groups, g_state, g_anchor, rate)
    factors = factors / groups
    e_avg = jnp.dot(factors, basis.T, precision=HIGHEST, preferred_element_type=jnp.float32)
    e_out = nesterov(e_avg, e_state, e_anchor, rate)
    return (*kv_out, *r_out, *g_out, *e_out)


IN_SPECS = (
    P("group", None, "dp", "tensor"),
    P(None, "dp", "tensor"),
    P(None, "dp", "tensor"),
    P("group", "dp", None),
    P("dp", None),
    P("dp", None),
    P("group", None, "dp"),
    P(None, "dp"),
    P(None, "dp"),
    P("group", "dp", "tensor"),
    P("dp", "tensor"),
    P("dp", "tensor"),
    P("tensor", None),
    P(),
)
OUT_SPECS = (
    P(None, "dp", "tensor"),
    P(None, "dp", "tensor"),
    P(None, "dp", "tensor"),
    P("dp", None),
    P("dp", None),
    P("dp", None),
    P(None, "dp"),
    P(None, "dp"),
    P(None, "dp"),
    P("dp", "tensor"),
    P("dp", "tensor"),
    P("dp", "tensor"),
)


def solution(mesh):
    return jax.shard_map(local, mesh=mesh, in_specs=IN_SPECS, out_specs=OUT_SPECS, check_vma=False)
```

profile of v0, /device:TPU:32, one launch (start us, length us, event | category | flops | bytes accessed | tf_op | source)
XLA Modules:
  0.0 108.0 jit_solution(13273733922246938453)
XLA Ops:
  7.2 0.0 copy-start
  7.2 0.0 all-reduce.3.cloned.1.call-start
  7.2 2.1 %bitcast_subtract_fusion = f32[2,512,128]{2,1,0:T(8,128)} fusion(f32[2,512,128]{2,1,0:T(8,128)} %param.15, f32[1,2,512,128]{3,2,1,0:T(8,128)} %param.14), kind=kLoop, calls=%fused_computation | loop fusion | flops 131072 | bytes 1572864 | tf_op jit(solution)/shard_map/sub | solution.py:33
  9.3 0.0 copy-start.2
  9.3 0.0 copy-start.4
  9.3 0.0 all-reduce.3.cloned.1.call-update
  10.0 0.0 copy-done
  10.1 0.2 copy-done.2
  10.3 0.1 copy-done.4
  10.4 0.0 copy-start.6
  10.4 0.0 copy-start.7
  10.4 0.0 copy-start.8
  10.4 0.0 copy-start.10
  10.4 0.4 fusion
  10.7 0.0 copy-start.5
  10.8 58.1 %psum.38 = f32[125,64]{1,0:T(8,128)S(1)} all-reduce(f32[125,64]{1,0:T(8,128)S(1)} %fusion), channel_id=1, replica_groups=mesh['group'=8,'dp'=8,'tensor'=8] {'tensor'}, use_global_device_ids=true, to_apply=%region_3.0 | all-reduce | flops 8000 | bytes 64000 | tf_op jit(solution)/shard_map/psum | solution.py:50
  68.9 0.0 copy-done.6
  68.9 0.0 copy-done.7
  68.9 0.0 copy-done.8
  68.9 0.0 copy-done.10
  68.9 0.0 copy-start.11
  68.9 27.3 %all-reduce = (f32[512,8]{0,1:T(8,128)S(1)}, f32[2,512]{1,0:T(2,128)S(1)}, f32[125,64]{1,0:T(8,128)S(1)}) all-reduce(f32[512,8]{0,1:T(8,128)S(1)} %bitcast_subtract_fusion.3, f32[2,512]{1,0:T(2,128)S(1)} %bitcast_subtract_fusion.4, f32[125,64]{1,0:T(8,128)S(1)} %psum.38), channel_id=1, replica_groups=mesh['group'=8,'dp'=8,'tensor'=8] {'group'}, use_global_device_ids=true, to_apply=%region_1.0 | all-reduce | flops 13120 | bytes 104960 | tf_op jit(solution)/shard_map/psum | solution.py:51
  96.3 0.0 copy-start.9
  96.3 0.0 copy-done.11
  96.3 0.6 multiply_subtract_fusion.3
  96.9 0.1 copy-done.9
  97.0 0.6 multiply_subtract_fusion.2
  97.6 0.0 copy-done.5
  97.6 0.0 copy-start.1
  97.6 0.0 copy-start.3
  97.6 1.3 %multiply_subtract_fusion.1 = (f32[125,512]{1,0:T(8,128)}, f32[125,512]{1,0:T(8,128)}, f32[125,512]{1,0:T(8,128)}) fusion(f32[125,512]{1,0:T(8,128)S(1)} %copy-done.2, f32[]{:T(128)S(6)} %copy.32, f32[125,512]{1,0:T(8,128)S(1)} %copy-done.5, f32[512,64]{0,1:T(8,128)S(1)} %copy-done, f32[125,64]{1,0:T(8,128)S(1)} %get-tuple-element.14), kind=kOutput, calls=%fused_computation.6 | convolution fusion | flops 49544000 | bytes 1443076 | tf_op jit(solution)/shard_map/dot_general | solution.py:59
  98.9 0.0 all-reduce.3.cloned.1.call-done
  98.9 0.0 copy-done.1
  98.9 0.0 copy-done.3
  98.9 2.3 %multiply_subtract_fusion = (f32[2,512,128]{2,1,0:T(8,128)}, f32[2,512,128]{2,1,0:T(8,128)}, f32[2,512,128]{2,1,0:T(8,128)}) fusion(f32[2,512,128]{2,1,0:T(8,128)S(1)} %copy-done.1, f32[]{:T(128)S(6)} %copy.32, f32[2,512,128]{2,1,0:T(8,128)S(1)} %copy-done.3, f32[2,512,128]{2,1,0:T(8,128)} %all-reduce.3.cloned.1.call-done), kind=kLoop, calls=%fused_computation.1 | loop fusion | flops 917504 | bytes 3145732 | tf_op jit(solution)/shard_map/sub | solution.py:12
  (2 shorter events, 0.0 us)
Async XLA Ops:
  7.2 2.9 %copy-start = (f32[512,64]{0,1:T(8,128)S(1)}, f32[512,64]{0,1:T(8,128)}, u32[]{:S(2)}) copy-start(f32[512,64]{0,1:T(8,128)} %param.26) | copy-start | bytes 393220
  7.2 91.7 %all-reduce.3.cloned.1.call-start = ((), (), s32[]{:S(2)}) async-start(), calls=%async_computation | async-start | bytes 1048576 | tf_op jit(solution)/shard_map/psum | solution.py:51
  9.3 1.0 copy-start.2
  9.3 1.0 copy-start.4
  10.4 58.5 %copy-start.6 = (f32[512,8]{0,1:T(8,128)S(1)}, f32[512,8]{0,1:T(8,128)}, u32[]{:S(2)}) copy-start(f32[512,8]{0,1:T(8,128)} %param.18) | copy-start | bytes 49156
  10.4 58.5 %copy-start.7 = (f32[1,512,8]{1,2,0:T(8,128)S(1)}, f32[1,512,8]{1,2,0:T(8,128)}, u32[]{:S(2)}) copy-start(f32[1,512,8]{1,2,0:T(8,128)} %param.17) | copy-start | bytes 49156
  10.4 58.5 %copy-start.8 = (f32[2,512]{1,0:T(2,128)S(1)}, f32[2,512]{1,0:T(2,128)}, u32[]{:S(2)}) copy-start(f32[2,512]{1,0:T(2,128)} %param.21) | copy-start | bytes 12292
  10.4 58.5 %copy-start.10 = (f32[1,2,512]{2,1,0:T(2,128)S(1)}, f32[1,2,512]{2,1,0:T(2,128)}, u32[]{:S(2)}) copy-start(f32[1,2,512]{2,1,0:T(2,128)} %param.20) | copy-start | bytes 12292
  10.7 86.9 %copy-start.5 = (f32[125,512]{1,0:T(8,128)S(1)}, f32[125,512]{1,0:T(8,128)}, u32[]{:S(2)}) copy-start(f32[125,512]{1,0:T(8,128)} %param.25) | copy-start | bytes 768004
  68.9 27.3 %copy-start.11 = (f32[2,512]{1,0:T(2,128)S(1)}, f32[2,512]{1,0:T(2,128)}, u32[]{:S(2)}) copy-start(f32[2,512]{1,0:T(2,128)} %param.22) | copy-start | bytes 12292
  96.3 0.7 copy-start.9
  97.6 1.3 %copy-start.1 = (f32[2,512,128]{2,1,0:T(8,128)S(1)}, f32[2,512,128]{2,1,0:T(8,128)}, u32[]{:S(2)}) copy-start(f32[2,512,128]{2,1,0:T(8,128)} %param.15) | copy-start | bytes 1572868
  97.6 1.3 %copy-start.3 = (f32[2,512,128]{2,1,0:T(8,128)S(1)}, f32[2,512,128]{2,1,0:T(8,128)}, u32[]{:S(2)}) copy-start(f32[2,512,128]{2,1,0:T(8,128)} %param.16) | copy-start | bytes 1572868
Sparse Core Ops, SparseCore 0:
  11.5 82.3 all-reduce.2
where the time goes:
time: 108 us
  blocking collectives  85.4 us (79%)
  between operations  14.9 us (14%)
  other arithmetic  5.61 us (5%)
  matrix products  1.64 us (2%)
    psum x1, blocking collectives, local(): partial = lax.psum(partial, 'tensor')  58.1 us
    psum x1, blocking collectives, local(): lax.psum((kv_diff, r_diff, g_diff, partial), 'group')  27.3 us
    sub x3, other arithmetic, nesterov(): updated = anchor - outer_rate * (average + 0.5 * momentum)  3.52 us
  transfers between devices with their start and end apart: 1, of which 0 were waited for; matrix products, arithmetic and copies ran while one was open for 3% of the time, Pallas kernels for 0%

commit v1 on v0

--- a/solution.py
+++ b/solution.py
@@ -47,7 +47,7 @@
             at += p.size
         kv_sum, r_sum, g_sum, factors = sums
     elif MODE == "separate":
-        partial = lax.psum(partial, "tensor")
+        partial = jnp.sum(lax.all_gather(partial, "tensor"), axis=0)
         kv_sum, r_sum, g_sum, factors = lax.psum((kv_diff, r_diff, g_diff, partial), "group")
     elif MODE == "nested":
         kv_sum, r_sum, g_sum = lax.psum((kv_diff, r_diff, g_diff), "group")

time: 108 us -> 105 us (0.972)
  the two profiles are of different devices: /device:TPU:32 before, /device:TPU:2 now
where the time goes in v1:
time: 105 us; the launch traced here: 104 us
  blocking collectives  74.4 us (71%)
  between operations  14.9 us (14%)
  waiting for transfers between devices  7.08 us (7%)
  other arithmetic  5.64 us (5%)
  matrix products  1.73 us (2%)
    all_gather x1, blocking collectives, local(): partial = jnp.sum(lax.all_gather(partial, 'tensor'), axis=0)  48 us
    psum x1, blocking collectives, local(): lax.psum((kv_diff, r_diff, g_diff, partial), 'group')  26.4 us
    psum x1, waiting for transfers between devices, local(): lax.psum((kv_diff, r_diff, g_diff, partial), 'group')  7.07 us
    sub x3, other arithmetic, nesterov(): updated = anchor - outer_rate * (average + 0.5 * momentum)  3.52 us
  transfers between devices with their start and end apart: 1, of which 1 were waited for; matrix products, arithmetic and copies ran while one was open for 3% of the time, Pallas kernels for 0%

profile of v1, /device:TPU:2, one launch (start us, length us, event | category | flops | bytes accessed | tf_op | source)
XLA Modules:
  0.0 104.2 jit_solution(14207348584325328699)
XLA Ops:
  7.2 0.0 copy-start
  7.2 0.0 all-reduce.3.cloned.1.call-start
  7.2 2.1 %bitcast_subtract_fusion = f32[2,512,128]{2,1,0:T(8,128)} fusion(f32[2,512,128]{2,1,0:T(8,128)} %param.15, f32[1,2,512,128]{3,2,1,0:T(8,128)} %param.14), kind=kLoop, calls=%fused_computation.1 | loop fusion | flops 131072 | bytes 1572864 | tf_op jit(solution)/shard_map/sub | solution.py:33
  9.3 0.0 copy-start.2
  9.3 0.0 copy-start.4
  9.3 0.0 all-reduce.3.cloned.1.call-update
  10.0 0.0 copy-done
  10.1 0.2 copy-done.2
  10.3 0.1 copy-done.4
  10.4 0.4 convolution_bitcast_fusion
  10.8 0.0 copy-start.6
  10.8 0.0 copy-start.7
  10.8 0.0 copy-start.8
  10.8 0.0 copy-start.10
  10.8 48.0 %all-gather.1 = f32[8,125,64]{1,2,0:T(8,128)S(1)} all-gather(f32[1,125,64]{1,2,0:T(8,128)S(1)} %convolution_bitcast_fusion), channel_id=2, replica_groups=mesh['group'=8,'dp'=8,'tensor'=8] {'tensor'}, dimensions={0}, use_global_device_ids=true | all-gather | bytes 288000 | tf_op jit(solution)/shard_map/all_gather | solution.py:50
  58.8 0.0 copy-done.6
  58.8 0.0 copy-done.7
  58.8 0.0 copy-start.5
  58.8 0.0 copy-done.8
  58.8 0.0 copy-done.10
  58.9 0.0 copy-start.11
  58.9 26.4 %all-reduce = (f32[512,8]{0,1:T(8,128)S(1)}, f32[2,512]{1,0:T(2,128)S(1)}, f32[125,64]{0,1:T(8,128)S(1)}) all-reduce(f32[512,8]{0,1:T(8,128)S(1)} %bitcast_subtract_fusion.3, f32[2,512]{1,0:T(2,128)S(1)} %bitcast_subtract_fusion.4, f32[125,64]{0,1:T(8,128)S(1)} %reduce_sum.9), channel_id=1, replica_groups=mesh['group'=8,'dp'=8,'tensor'=8] {'group'}, use_global_device_ids=true, to_apply=%region_1.0 | all-reduce | flops 13120 | bytes 104960 | tf_op jit(solution)/shard_map/psum | solution.py:51
  85.3 0.0 copy-start.9
  85.3 0.0 copy-done.11
  85.3 0.6 multiply_subtract_fusion.3
  85.9 0.1 copy-done.9
  86.0 0.6 multiply_subtract_fusion.2
  86.6 0.0 copy-done.5
  86.6 0.0 copy-start.1
  86.6 0.0 copy-start.3
  86.6 1.3 %multiply_subtract_fusion.1 = (f32[125,512]{1,0:T(8,128)}, f32[125,512]{1,0:T(8,128)}, f32[125,512]{1,0:T(8,128)}) fusion(f32[125,512]{1,0:T(8,128)S(1)} %copy-done.2, f32[]{:T(128)S(6)} %copy.32, f32[125,512]{1,0:T(8,128)S(1)} %copy-done.5, f32[512,64]{0,1:T(8,128)S(1)} %copy-done, f32[125,64]{0,1:T(8,128)S(1)} %get-tuple-element.14), kind=kOutput, calls=%fused_computation.6 | convolution fusion | flops 49544000 | bytes 1443076 | tf_op jit(solution)/shard_map/dot_general | solution.py:59
  88.0 7.1 %all-reduce.3.cloned.1.call-done = f32[2,512,128]{2,1,0:T(8,128)} async-done(((f32[2,512,128]{2,1,0:T(8,128)}), f32[2,512,128]{2,1,0:T(8,128)}) %all-reduce.3.cloned.1.call-update) | async-done | bytes 524304 | tf_op jit(solution)/shard_map/psum | solution.py:51
  95.0 0.0 copy-done.1
  95.0 0.0 copy-done.3
  95.0 2.3 %multiply_subtract_fusion = (f32[2,512,128]{2,1,0:T(8,128)}, f32[2,512,128]{2,1,0:T(8,128)}, f32[2,512,128]{2,1,0:T(8,128)}) fusion(f32[2,512,128]{2,1,0:T(8,128)S(1)} %copy-done.1, f32[]{:T(128)S(6)} %copy.32, f32[2,512,128]{2,1,0:T(8,128)S(1)} %copy-done.3, f32[2,512,128]{2,1,0:T(8,128)} %all-reduce.3.cloned.1.call-done), kind=kLoop, calls=%fused_computation.2 | loop fusion | flops 917504 | bytes 3145732 | tf_op jit(solution)/shard_map/sub | solution.py:12
  (3 shorter events, 0.0 us)
Async XLA Ops:
  7.2 2.9 %copy-start = (f32[512,64]{0,1:T(8,128)S(1)}, f32[512,64]{0,1:T(8,128)}, u32[]{:S(2)}) copy-start(f32[512,64]{0,1:T(8,128)} %param.26) | copy-start | bytes 393220
  7.2 87.8 %all-reduce.3.cloned.1.call-start = ((), (), s32[]{:S(2)}) async-start(), calls=%async_computation | async-start | bytes 1048576 | tf_op jit(solution)/shard_map/psum | solution.py:51
  9.3 1.0 copy-start.2
  9.3 1.0 copy-start.4
  10.8 48.1 %copy-start.6 = (f32[512,8]{0,1:T(8,128)S(1)}, f32[512,8]{0,1:T(8,128)}, u32[]{:S(2)}) copy-start(f32[512,8]{0,1:T(8,128)} %param.18) | copy-start | bytes 49156
  10.8 48.0 %copy-start.7 = (f32[1,512,8]{1,2,0:T(8,128)S(1)}, f32[1,512,8]{1,2,0:T(8,128)}, u32[]{:S(2)}) copy-start(f32[1,512,8]{1,2,0:T(8,128)} %param.17) | copy-start | bytes 49156
  10.8 48.1 %copy-start.8 = (f32[2,512]{1,0:T(2,128)S(1)}, f32[2,512]{1,0:T(2,128)}, u32[]{:S(2)}) copy-start(f32[2,512]{1,0:T(2,128)} %param.21) | copy-start | bytes 12292
  10.8 48.1 %copy-start.10 = (f32[1,2,512]{2,1,0:T(2,128)S(1)}, f32[1,2,512]{2,1,0:T(2,128)}, u32[]{:S(2)}) copy-start(f32[1,2,512]{2,1,0:T(2,128)} %param.20) | copy-start | bytes 12292
  58.8 27.8 %copy-start.5 = (f32[125,512]{1,0:T(8,128)S(1)}, f32[125,512]{1,0:T(8,128)}, u32[]{:S(2)}) copy-start(f32[125,512]{1,0:T(8,128)} %param.25) | copy-start | bytes 768004
  58.9 26.4 %copy-start.11 = (f32[2,512]{1,0:T(2,128)S(1)}, f32[2,512]{1,0:T(2,128)}, u32[]{:S(2)}) copy-start(f32[2,512]{1,0:T(2,128)} %param.22) | copy-start | bytes 12292
  85.3 0.7 copy-start.9
  86.6 8.4 %copy-start.1 = (f32[2,512,128]{2,1,0:T(8,128)S(1)}, f32[2,512,128]{2,1,0:T(8,128)}, u32[]{:S(2)}) copy-start(f32[2,512,128]{2,1,0:T(8,128)} %param.15) | copy-start | bytes 1572868
  86.6 8.4 %copy-start.3 = (f32[2,512,128]{2,1,0:T(8,128)S(1)}, f32[2,512,128]{2,1,0:T(8,128)}, u32[]{:S(2)}) copy-start(f32[2,512,128]{2,1,0:T(8,128)} %param.16) | copy-start | bytes 1572868
Sparse Core Ops, SparseCore 0:
  11.5 83.4 all-reduce.2
